TPU v7x, 32 devices: a whole 2x2x4 slice. The times are simulated.
32 devices in a mesh: gx: 8 (over z, y), gy: 4 (over x, core).
Axes of the slice: x: 2, y: 2, z: 4, core: 2. Of those that a mesh axis runs over, the one named last changes fastest.
Arguments:
- conc_prev: float32 [128, 64, 128], P('gx', 'gy'), may hold values from 0.5 to 2
- right_side: float32 [128, 64, 128], P('gx', 'gy'), may hold values from -5 to 7
- soil_id: int32 [128, 64, 128], P('gx', 'gy'), may hold values from 0 to 7
- soil_table: float32 [5, 8], replicated, may hold values from 0.3 to 3
Outputs:
- correction: float32 [128, 64, 128], P('gx', 'gy')
All inputs are finite; a program needn't handle non-finite values.
Results may differ from a plain program's by a relative error of at most 0.00002.
Values sent between devices are 32-bit elements; how exact they have to be, the bound alone decides.
No kernel may reach another device: no remote copies, remote signals or barrier semaphores. Data moves between devices by JAX's collectives and lax.ppermute only.
A program may use at most 128 MiB of HBM per device.

v0:
```python
import jax
import jax.numpy as jnp
from jax import lax
from jax.sharding import PartitionSpec as P

CHEB = 3
COARSE_SWEEPS = 8
storage_scale = 0.05
cheb_centre = 1.1
cheb_half = 0.9
cheb_ratio = cheb_centre / cheb_half
jacobi_weight = 0.8


def padded_2(cells, sides, width):
    for axis, dim in sides:
        count = lax.axis_size(axis)
        ends = count - 1
        head = lax.slice_in_dim(cells, 0, width, axis=dim)
        tail = lax.slice_in_dim(cells, cells.shape[dim] - width, cells.shape[dim], axis=dim)
        cells = jnp.concatenate(
            [
                lax.ppermute(tail, axis, [(i, (i + 1) % count) for i in range(ends)]),
                cells,
                lax.ppermute(head, axis, [((i + 1) % count, i) for i in range(ends)]),
            ],
            axis=dim,
        )
    return cells


def harmonic(first, second):
    return first * second / jnp.maximum(0.5 * (first + second), 0.1)


def face_terms(coeffs, spacing):
    eastward = coeffs[0]
    northward = coeffs[1]
    upward = coeffs[2]
    centre_x = eastward[1:-1, 1:-1]
    centre_y = northward[1:-1, 1:-1]
    centre_z = upward[1:-1, 1:-1]
    east_face = harmonic(eastward[2:, 1:-1], centre_x) * spacing
    west_face = harmonic(eastward[:-2, 1:-1], centre_x) * spacing
    north_face = harmonic(northward[1:-1, 2:], centre_y) * spacing
    south_face = harmonic(northward[1:-1, :-2], centre_y) * spacing
    vertical = harmonic(centre_z[:, :, 1:], centre_z[:, :, :-1]) * spacing
    closed = jnp.zeros_like(centre_z[:, :, :1])
    above_face = jnp.concatenate([vertical, closed], axis=2)
    below_face = jnp.concatenate([closed, vertical], axis=2)
    storage = coeffs[3, 1:-1, 1:-1]
    return (east_face, west_face, north_face, south_face, above_face, below_face, storage)


def main_diagonal(coeffs, spacing):
    east_face, west_face, north_face, south_face, above_face, below_face, storage = face_terms(
        coeffs, spacing
    )
    return jnp.maximum(
        storage + east_face + west_face + north_face + south_face + above_face + below_face, 0.01
    )


def operate(values, coeffs, spacing):
    east_face, west_face, north_face, south_face, above_face, below_face, storage = face_terms(
        coeffs, spacing
    )
    centre = values[1:-1, 1:-1]
    upper_cell = jnp.concatenate([centre[:, :, 1:], centre[:, :, :1]], axis=2)
    lower_cell = jnp.concatenate([centre[:, :, -1:], centre[:, :, :-1]], axis=2)
    fluxes = east_face * (centre - values[2:, 1:-1]) + west_face * (centre - values[:-2, 1:-1])
    fluxes = (
        fluxes
        + north_face * (centre - values[1:-1, 2:])
        + south_face * (centre - values[1:-1, :-2])
    )
    fluxes = fluxes + above_face * (centre - upper_cell) + below_face * (centre - lower_cell)
    return storage * centre + fluxes


def coarsen(values):
    lead = values.shape[:-3]
    size_x, size_y, size_z = values.shape[-3:]
    split = values.reshape(lead + (size_x // 2, 2, size_y // 2, 2, size_z // 2, 2))
    return jnp.mean(split, axis=(-5, -3, -1))


def prolong(values):
    return jnp.repeat(jnp.repeat(jnp.repeat(values, 2, axis=0), 2, axis=1), 2, axis=2)


def shrink(values, amount):
    if amount == 0:
        return values
    return values[..., amount:-amount, amount:-amount, :]


def tile_halo(layers, amount):
    return padded_2(layers, (("gx", 1), ("gy", 2)), amount)


def expand(values):
    return (tile_halo(values[None], 1)[0], 1)


def smooth(target, target_margin, initial, coeffs, coeff_margin, spacing):
    if initial is None:
        current = target_margin
        diagonal = main_diagonal(shrink(coeffs, coeff_margin - current - 1), spacing)
        update = target / diagonal * (1.0 / cheb_centre)
        iterate = update
    else:
        padded, padded_margin = expand(initial)
        applied = operate(padded, shrink(coeffs, coeff_margin - padded_margin), spacing)
        current = padded_margin - 1
        diagonal = main_diagonal(shrink(coeffs, coeff_margin - current - 1), spacing)
        misfit = shrink(target, target_margin - current) - applied
        update = misfit / diagonal * (1.0 / cheb_centre)
        iterate = shrink(padded, 1) + update
    diagonal_margin = current
    factor = 1.0 / cheb_ratio
    for repeat in range(CHEB - 1):
        padded, padded_margin = expand(iterate)
        applied = operate(padded, shrink(coeffs, coeff_margin - padded_margin), spacing)
        next_margin = padded_margin - 1
        misfit = shrink(target, target_margin - next_margin) - applied
        factor_new = 1.0 / (2.0 * cheb_ratio - factor)
        update = factor_new * factor * shrink(
            update, current - next_margin
        ) + 2.0 * factor_new / cheb_half * (
            misfit / shrink(diagonal, diagonal_margin - next_margin)
        )
        iterate = shrink(iterate, current - next_margin) + update
        current = next_margin
        factor = factor_new
    return (iterate, current)


def leftover(target, target_margin, iterate, coeffs, coeff_margin, spacing):
    padded, padded_margin = expand(iterate)
    applied = operate(padded, shrink(coeffs, coeff_margin - padded_margin), spacing)
    return shrink(target, target_margin - padded_margin + 1) - applied


def local_fields(conc_prev, soil_id, soil_table):
    fields = []
    for record in range(5):
        looked = jnp.zeros(soil_id.shape, jnp.float32)
        for material in range(soil_table.shape[1]):
            looked = looked + jnp.where(soil_id == material, soil_table[record, material], 0.0)
        fields.append(looked)
    storage = storage_scale * (1.0 + fields[3] * jnp.exp((fields[4] - 1.0) * jnp.log(conc_prev)))
    return jnp.stack([fields[0], fields[1], fields[2], storage])


def local(conc_prev, right_side, soil_id, soil_table):
    halo_depth = 0
    fine_margin = max(4, 2 * halo_depth + 2)
    own_coeffs = local_fields(conc_prev, soil_id, soil_table)
    fine_coeffs = padded_2(own_coeffs, (("gx", 1), ("gy", 2)), fine_margin)
    mid_margin = fine_margin // 2
    mid_coeffs = coarsen(fine_coeffs)
    coarse_coeffs = coarsen(shrink(mid_coeffs, mid_margin - 2))
    fine_iterate, current = smooth(right_side, halo_depth, None, fine_coeffs, fine_margin, 1.0)
    fine_misfit = leftover(right_side, halo_depth, fine_iterate, fine_coeffs, fine_margin, 1.0)
    fine_iterate = shrink(fine_iterate, current)
    mid_plain = coarsen(fine_misfit)
    mid_iterate, current = smooth(mid_plain, halo_depth, None, mid_coeffs, mid_margin, 0.25)
    mid_misfit = leftover(mid_plain, halo_depth, mid_iterate, mid_coeffs, mid_margin, 0.25)
    mid_iterate = shrink(mid_iterate, current)
    coarse_source = coarsen(mid_misfit)
    narrow = coarse_coeffs[:, :, 1:-1]
    group_source, group_coeffs = (
        lax.all_gather(coarse_source, "gy", axis=1, tiled=True),
        lax.all_gather(narrow, "gy", axis=2, tiled=True),
    )
    line_total = jnp.sum(group_source, axis=1)
    line_store = jnp.sum(group_coeffs[3, 1:-1], axis=1)
    line_mean = line_total / line_store
    group_coeffs = jnp.pad(group_coeffs, ((0, 0), (0, 0), (1, 1), (0, 0)))
    diagonal = main_diagonal(group_coeffs, 0.0625)
    coarse_value = jnp.broadcast_to(line_mean[:, None, :], group_source.shape)
    for sweeps in range(COARSE_SWEEPS):
        padded = padded_2(coarse_value, (("gx", 0),), 1)
        padded = jnp.pad(padded, ((0, 0), (1, 1), (0, 0)))
        applied = operate(padded, group_coeffs, 0.0625)
        coarse_value = coarse_value + jacobi_weight * ((group_source - applied) / diagonal)
    tile_width = coarse_source.shape[1]
    coarse_value = lax.dynamic_slice_in_dim(
        coarse_value, lax.axis_index("gy") * tile_width, tile_width, 1
    )
    mid_start = mid_iterate + prolong(coarse_value)
    mid_result, current = smooth(mid_plain, halo_depth, mid_start, mid_coeffs, mid_margin, 0.25)
    fine_start = fine_iterate + prolong(mid_result)
    fine_result, current = smooth(right_side, halo_depth, fine_start, fine_coeffs, fine_margin, 1.0)
    return fine_result


def solution(mesh):
    placed = (P("gx", "gy", None), P("gx", "gy", None), P("gx", "gy", None), P())
    return jax.shard_map(
        local, mesh=mesh, in_specs=placed, out_specs=P("gx", "gy", None), check_vma=False
    )
```

profile of v0, /device:TPU:26, one launch (start us, length us, event | category | flops | bytes accessed | tf_op | source)
XLA Modules:
  0.0 402.7 jit_solution(15851466285160394497)
XLA Ops:
  5.6 6.3 %add_bitcast_fusion.3 = (f32[1,16,16,128]{3,2,1,0:T(8,128)S(1)}, pred[16,16,128]{2,1,0:T(8,128)(4,1)S(1)}, pred[16,16,128]{2,1,0:T(8,128)(4,1)S(1)}, pred[16,16,...) fusion(f32[]{:T(128)} %bitcast.23, f32[]{:T(128)} %bitcast.22, ...), kind=kLoop, calls=%fused_computation.162 | loop fusion | flops 753664 | bytes 524320 | tf_op jit(solution)/shard_map/stack | solution.py:153
  11.9 5.3 %add_bitcast_fusion.1 = f32[1,16,16,128]{3,2,1,0:T(8,128)S(1)} fusion(pred[16,16,128]{2,1,0:T(8,128)(4,1)S(1)} %get-tuple-element.49, pred[16,16,128]{2,1,0:T(8,128)(4,1)S(1)} %get-tuple-element.48, pred[16,16,128]{2,1,0:T(8,128)(4,1)S(1)} %get-tuple-element.47, pred[16,16,128]{2,1,0:T(8,128)(4,1)S(1)} %get-tuple-element.46, ...), kind=kLoop, calls=%fused_computation.160 | loop fusion | flops 491520 | bytes 393248 | tf_op jit(solution)/shard_map/stack | solution.py:153
  17.2 5.0 %add_bitcast_fusion.2 = f32[1,16,16,128]{3,2,1,0:T(8,128)S(1)} fusion(pred[16,16,128]{2,1,0:T(8,128)(4,1)S(1)} %get-tuple-element.49, pred[16,16,128]{2,1,0:T(8,128)(4,1)S(1)} %get-tuple-element.48, pred[16,16,128]{2,1,0:T(8,128)(4,1)S(1)} %get-tuple-element.47, pred[16,16,128]{2,1,0:T(8,128)(4,1)S(1)} %get-tuple-element.46, ...), kind=kLoop, calls=%fused_computation.161 | loop fusion | flops 491520 | bytes 393248 | tf_op jit(solution)/shard_map/stack | solution.py:153
  22.1 10.1 %add_multiply_fusion = f32[16,16,128]{2,1,0:T(8,128)S(1)} fusion(f32[16,16,128]{2,1,0:T(8,128)S(1)} %copy-done.1, pred[16,16,128]{2,1,0:T(8,128)(4,1)S(1)} %get-tuple-element.49, pred[16,16,128]{2,1,0:T(8,128)(4,1)S(1)} %get-tuple-element.48, pred[16,16,128]{2,1,0:T(8,128)(4,1)S(1)} %get-tuple-element.47, pred[16,16,128]{2,1,0:T(8,128)(4,1)S(1)} %get-tuple-element.46, ...), kind=kLoop, calls=%fused_computation.163 | loop fusion | flops 1146880 | bytes 524352 | tf_op jit(solution)/shard_map/mul | solution.py:152
  39.5 4.0 collective-permute-done
  72.8 3.9 collective-permute-start.8
  76.7 18.2 %copy.868 = f32[4,24,24,128]{0,3,2,1:T(8,128)} copy(f32[4,24,24,128]{3,2,1,0:T(8,128)S(1)} %pad_maximum_fusion) | data formatting | bytes 2359296 | tf_op jit(solution)/shard_map/concatenate | solution.py:21
  94.9 27.0 %reduce_sum.55 = f32[4,12,12,64]{0,3,2,1:T(8,128)} reduce(f32[4,12,2,12,2,64,2]{0,6,5,4,3,2,1:T(2,128)} %bitcast.161, f32[]{:T(128)} %constant.27.clone.1), dimensions={2,4,6}, to_apply=%region_1.2 | reduce | flops 258048 | bytes 1327108 | tf_op jit(solution)/shard_map/reduce_sum | solution.py:85
  149.8 9.8 %reshape.56 = f32[8,2,8,2,64,2]{5,4,3,2,1,0:T(8,128)} reshape(f32[16,16,128]{2,1,0:T(8,128)S(1)} %fusion.41) | data formatting | bytes 262144 | tf_op jit(solution)/shard_map/reshape | solution.py:84
  159.6 4.0 reduce_sum.54
  165.7 4.0 collective-permute-start.16
  172.8 5.3 %reduce_sum.58 = f32[4,6,6,32]{0,3,2,1:T(8,128)S(1)} reduce(f32[4,6,2,6,2,32,2]{0,6,5,4,3,2,1:T(2,128)} %bitcast.162, f32[]{:T(128)} %constant.27.clone.1), dimensions={2,4,6}, to_apply=%region_4.5 | reduce | flops 32256 | bytes 165892 | tf_op jit(solution)/shard_map/reduce_sum | solution.py:85
  191.3 10.7 %all_gather.7 = f32[4,6,16,32]{0,3,2,1:T(8,128)S(1)} all-gather(f32[4,6,4,32]{0,3,2,1:T(8,128)S(1)} %slice_multiply_fusion), channel_id=1, replica_groups=mesh['gx'=8,'gy'=4] {'gy'}, dimensions={2}, use_global_device_ids=true | all-gather | bytes 61440 | tf_op jit(solution)/shard_map/all_gather | solution.py:175
  202.0 4.6 %collective-permute-start.23 = (f32[1,10,1,64]{3,2,1,0:T(1,128)S(1)}, f32[1,10,1,64]{3,2,1,0:T(1,128)S(1)}, u32[]{:S(2)}, u32[]{:S(2)}) collective-permute-start(f32[1,10,1,64]{3,2,1,0:T(1,128)S(1)} %get-tuple-element.143), channel_id=1, source_target_pairs={{1,0},{2,1},{3,2},{5,4},{6,5},{7,6},{9,8},{10,9},{11,10},{13,12},{... | collective-permute-start | bytes 7688 | tf_op jit(solution)/shard_map/ppermute | solution.py:25
  217.9 4.3 %collective-permute-done.24 = f32[1,1,8,64]{3,2,1,0:T(8,128)S(1)} collective-permute-done((f32[1,1,8,64]{3,2,1,0:T(8,128)S(1)}, f32[1,1,8,64]{3,2,1,0:T(8,128)S(1)}, u32[]{:S(2)}, u32[]{:S(2)}) %collective-permute-start.24) | collective-permute-done | bytes 2080 | tf_op jit(solution)/shard_map/ppermute | solution.py:23
  230.6 5.2 %all_gather.6 = f32[4,16,32]{2,0,1:T(4,128)S(1)} all-gather(f32[4,4,32]{2,0,1:T(4,128)S(1)} %copy.879), channel_id=1, replica_groups=mesh['gx'=8,'gy'=4] {'gy'}, dimensions={1}, use_global_device_ids=true | all-gather | bytes 10240 | tf_op jit(solution)/shard_map/all_gather | solution.py:174
  237.9 3.9 collective-permute-start.29
  256.2 3.9 collective-permute-start.33
  274.2 3.9 collective-permute-start.37
  300.1 3.9 collective-permute-start.43
  309.0 3.9 collective-permute-start.44
  324.5 3.9 collective-permute-start.48
  356.6 3.9 collective-permute-start.56
  372.4 3.9 collective-permute-start.60
  (303 shorter events, 242.2 us)
Async XLA Ops:
  32.3 7.1 %collective-permute-start.1 = (f32[4,4,16,128]{3,2,1,0:T(8,128)S(1)}, f32[4,4,16,128]{3,2,1,0:T(8,128)S(1)}, u32[]{:S(2)}, u32[]{:S(2)}) collective-permute-start(f32[4,4,16,128]{3,2,1,0:T(8,128)S(1)} %get-tuple-element.56), channel_id=1, source_target_pairs={{4,0},{8,4},{12,8},{16,12},{20,16},{24,20},{28,24},{5,1},{9,5},{13... | collective-permute-start | bytes 393224 | tf_op jit(solution)/shard_map/ppermute | solution.py:25
  35.6 7.8 %collective-permute-start = (f32[4,4,16,128]{3,2,1,0:T(8,128)S(1)}, f32[4,4,16,128]{3,2,1,0:T(8,128)S(1)}, u32[]{:S(2)}, u32[]{:S(2)}) collective-permute-start(f32[4,4,16,128]{3,2,1,0:T(8,128)S(1)} %get-tuple-element.55), channel_id=1, source_target_pairs={{0,4},{4,8},{8,12},{12,16},{16,20},{20,24},{24,28},{1,5},{5,9},{9,... | collective-permute-start | bytes 393224 | tf_op jit(solution)/shard_map/ppermute | solution.py:23
  45.5 7.0 %collective-permute-start.2 = (f32[4,24,4,128]{3,1,2,0:T(8,128)S(1)}, f32[4,24,4,128]{3,1,2,0:T(8,128)S(1)}, u32[]{:S(2)}, u32[]{:S(2)}) collective-permute-start(f32[4,24,4,128]{3,1,2,0:T(8,128)S(1)} %copy.912), channel_id=1, source_target_pairs={{0,1},{1,2},{2,3},{4,5},{5,6},{6,7},{8,9},{9,10},{10,11},{12,13},{... | collective-permute-start | bytes 589832 | tf_op jit(solution)/shard_map/ppermute | solution.py:23
  57.0 6.4 %collective-permute-start.4 = (f32[1,1,16,128]{3,2,1,0:T(8,128)S(1)}, f32[1,1,16,128]{3,2,1,0:T(8,128)S(1)}, u32[]{:S(2)}, u32[]{:S(2)}) collective-permute-start(f32[1,1,16,128]{3,2,1,0:T(8,128)S(1)} %get-tuple-element.108), channel_id=1, source_target_pairs={{0,4},{4,8},{8,12},{12,16},{16,20},{20,24},{24,28},{1,5},{5,9},{9,... | collective-permute-start | bytes 24584 | tf_op jit(solution)/shard_map/ppermute | solution.py:23
  70.9 54.8 %collective-permute-start.9 = (f32[1,1,16,128]{3,2,1,0:T(8,128)S(1)}, f32[1,1,16,128]{3,2,1,0:T(8,128)S(1)}, u32[]{:S(2)}, u32[]{:S(2)}) collective-permute-start(f32[1,1,16,128]{3,2,1,0:T(8,128)S(1)} %get-tuple-element.107), channel_id=1, source_target_pairs={{4,0},{8,4},{12,8},{16,12},{20,16},{24,20},{28,24},{5,1},{9,5},{13... | collective-permute-start | bytes 24584 | tf_op jit(solution)/shard_map/ppermute | solution.py:25
  72.8 52.9 %collective-permute-start.8 = (f32[1,1,16,128]{3,2,1,0:T(8,128)S(1)}, f32[1,1,16,128]{3,2,1,0:T(8,128)S(1)}, u32[]{:S(2)}, u32[]{:S(2)}) collective-permute-start(f32[1,1,16,128]{3,2,1,0:T(8,128)S(1)} %get-tuple-element.106), channel_id=1, source_target_pairs={{0,4},{4,8},{8,12},{12,16},{16,20},{20,24},{24,28},{1,5},{5,9},{9,... | collective-permute-start | bytes 24584 | tf_op jit(solution)/shard_map/ppermute | solution.py:23
  136.0 6.4 %collective-permute-start.12 = (f32[1,1,16,128]{3,2,1,0:T(8,128)S(1)}, f32[1,1,16,128]{3,2,1,0:T(8,128)S(1)}, u32[]{:S(2)}, u32[]{:S(2)}) collective-permute-start(f32[1,1,16,128]{3,2,1,0:T(8,128)S(1)} %get-tuple-element.104), channel_id=1, source_target_pairs={{0,4},{4,8},{8,12},{12,16},{16,20},{20,24},{24,28},{1,5},{5,9},{9,... | collective-permute-start | bytes 24584 | tf_op jit(solution)/shard_map/ppermute | solution.py:23
  163.7 14.5 %collective-permute-start.17 = (f32[1,1,8,64]{3,2,1,0:T(8,128)S(1)}, f32[1,1,8,64]{3,2,1,0:T(8,128)S(1)}, u32[]{:S(2)}, u32[]{:S(2)}) collective-permute-start(f32[1,1,8,64]{3,2,1,0:T(8,128)S(1)} %get-tuple-element.201), channel_id=1, source_target_pairs={{4,0},{8,4},{12,8},{16,12},{20,16},{24,20},{28,24},{5,1},{9,5},{13... | collective-permute-start | bytes 6152 | tf_op jit(solution)/shard_map/ppermute | solution.py:25
  165.7 12.5 %collective-permute-start.16 = (f32[1,1,8,64]{3,2,1,0:T(8,128)S(1)}, f32[1,1,8,64]{3,2,1,0:T(8,128)S(1)}, u32[]{:S(2)}, u32[]{:S(2)}) collective-permute-start(f32[1,1,8,64]{3,2,1,0:T(8,128)S(1)} %get-tuple-element.200), channel_id=1, source_target_pairs={{0,4},{4,8},{8,12},{12,16},{16,20},{20,24},{24,28},{1,5},{5,9},{9,... | collective-permute-start | bytes 6152 | tf_op jit(solution)/shard_map/ppermute | solution.py:23
  185.5 16.6 %collective-permute-start.21 = (f32[1,1,8,64]{3,2,1,0:T(8,128)S(1)}, f32[1,1,8,64]{3,2,1,0:T(8,128)S(1)}, u32[]{:S(2)}, u32[]{:S(2)}) collective-permute-start(f32[1,1,8,64]{3,2,1,0:T(8,128)S(1)} %get-tuple-element.199), channel_id=1, source_target_pairs={{4,0},{8,4},{12,8},{16,12},{20,16},{24,20},{28,24},{5,1},{9,5},{13... | collective-permute-start | bytes 6152 | tf_op jit(solution)/shard_map/ppermute | solution.py:25
  188.4 13.6 %collective-permute-start.20 = (f32[1,1,8,64]{3,2,1,0:T(8,128)S(1)}, f32[1,1,8,64]{3,2,1,0:T(8,128)S(1)}, u32[]{:S(2)}, u32[]{:S(2)}) collective-permute-start(f32[1,1,8,64]{3,2,1,0:T(8,128)S(1)} %get-tuple-element.198), channel_id=1, source_target_pairs={{0,4},{4,8},{8,12},{12,16},{16,20},{20,24},{24,28},{1,5},{5,9},{9,... | collective-permute-start | bytes 6152 | tf_op jit(solution)/shard_map/ppermute | solution.py:23
  202.0 8.8 %collective-permute-start.23 = (f32[1,10,1,64]{3,2,1,0:T(1,128)S(1)}, f32[1,10,1,64]{3,2,1,0:T(1,128)S(1)}, u32[]{:S(2)}, u32[]{:S(2)}) collective-permute-start(f32[1,10,1,64]{3,2,1,0:T(1,128)S(1)} %get-tuple-element.143), channel_id=1, source_target_pairs={{1,0},{2,1},{3,2},{5,4},{6,5},{7,6},{9,8},{10,9},{11,10},{13,12},{... | collective-permute-start | bytes 7688 | tf_op jit(solution)/shard_map/ppermute | solution.py:25
  215.7 6.4 %collective-permute-start.24 = (f32[1,1,8,64]{3,2,1,0:T(8,128)S(1)}, f32[1,1,8,64]{3,2,1,0:T(8,128)S(1)}, u32[]{:S(2)}, u32[]{:S(2)}) collective-permute-start(f32[1,1,8,64]{3,2,1,0:T(8,128)S(1)} %get-tuple-element.196), channel_id=1, source_target_pairs={{0,4},{4,8},{8,12},{12,16},{16,20},{20,24},{24,28},{1,5},{5,9},{9,... | collective-permute-start | bytes 6152 | tf_op jit(solution)/shard_map/ppermute | solution.py:23
  237.9 6.4 %collective-permute-start.29 = (f32[1,16,32]{2,1,0:T(8,128)S(1)}, f32[1,16,32]{2,1,0:T(8,128)S(1)}, u32[]{:S(2)}, u32[]{:S(2)}) collective-permute-start(f32[1,16,32]{2,1,0:T(8,128)S(1)} %broadcast_in_dim.285), channel_id=1, source_target_pairs={{0,4},{4,8},{8,12},{12,16},{16,20},{20,24},{24,28},{1,5},{5,9},{9,... | collective-permute-start | bytes 6152 | tf_op jit(solution)/shard_map/ppermute | solution.py:23
  247.6 6.4 %collective-permute-start.31 = (f32[1,16,32]{2,1,0:T(8,128)S(1)}, f32[1,16,32]{2,1,0:T(8,128)S(1)}, u32[]{:S(2)}, u32[]{:S(2)}) collective-permute-start(f32[1,16,32]{2,1,0:T(8,128)S(1)} %get-tuple-element.190), channel_id=1, source_target_pairs={{0,4},{4,8},{8,12},{12,16},{16,20},{20,24},{24,28},{1,5},{5,9},{9,... | collective-permute-start | bytes 6152 | tf_op jit(solution)/shard_map/ppermute | solution.py:23
  256.2 6.4 %collective-permute-start.33 = (f32[1,16,32]{2,1,0:T(8,128)S(1)}, f32[1,16,32]{2,1,0:T(8,128)S(1)}, u32[]{:S(2)}, u32[]{:S(2)}) collective-permute-start(f32[1,16,32]{2,1,0:T(8,128)S(1)} %get-tuple-element.184), channel_id=1, source_target_pairs={{0,4},{4,8},{8,12},{12,16},{16,20},{20,24},{24,28},{1,5},{5,9},{9,... | collective-permute-start | bytes 6152 | tf_op jit(solution)/shard_map/ppermute | solution.py:23
  265.7 6.4 %collective-permute-start.35 = (f32[1,16,32]{2,1,0:T(8,128)S(1)}, f32[1,16,32]{2,1,0:T(8,128)S(1)}, u32[]{:S(2)}, u32[]{:S(2)}) collective-permute-start(f32[1,16,32]{2,1,0:T(8,128)S(1)} %get-tuple-element.178), channel_id=1, source_target_pairs={{0,4},{4,8},{8,12},{12,16},{16,20},{20,24},{24,28},{1,5},{5,9},{9,... | collective-permute-start | bytes 6152 | tf_op jit(solution)/shard_map/ppermute | solution.py:23
  274.2 6.4 %collective-permute-start.37 = (f32[1,16,32]{2,1,0:T(8,128)S(1)}, f32[1,16,32]{2,1,0:T(8,128)S(1)}, u32[]{:S(2)}, u32[]{:S(2)}) collective-permute-start(f32[1,16,32]{2,1,0:T(8,128)S(1)} %get-tuple-element.172), channel_id=1, source_target_pairs={{0,4},{4,8},{8,12},{12,16},{16,20},{20,24},{24,28},{1,5},{5,9},{9,... | collective-permute-start | bytes 6152 | tf_op jit(solution)/shard_map/ppermute | solution.py:23
  282.8 6.4 %collective-permute-start.39 = (f32[1,16,32]{2,1,0:T(8,128)S(1)}, f32[1,16,32]{2,1,0:T(8,128)S(1)}, u32[]{:S(2)}, u32[]{:S(2)}) collective-permute-start(f32[1,16,32]{2,1,0:T(8,128)S(1)} %get-tuple-element.166), channel_id=1, source_target_pairs={{0,4},{4,8},{8,12},{12,16},{16,20},{20,24},{24,28},{1,5},{5,9},{9,... | collective-permute-start | bytes 6152 | tf_op jit(solution)/shard_map/ppermute | solution.py:23
  291.4 6.4 %collective-permute-start.41 = (f32[1,16,32]{2,1,0:T(8,128)S(1)}, f32[1,16,32]{2,1,0:T(8,128)S(1)}, u32[]{:S(2)}, u32[]{:S(2)}) collective-permute-start(f32[1,16,32]{2,1,0:T(8,128)S(1)} %get-tuple-element.160), channel_id=1, source_target_pairs={{0,4},{4,8},{8,12},{12,16},{16,20},{20,24},{24,28},{1,5},{5,9},{9,... | collective-permute-start | bytes 6152 | tf_op jit(solution)/shard_map/ppermute | solution.py:23
  300.1 6.4 %collective-permute-start.43 = (f32[1,16,32]{2,1,0:T(8,128)S(1)}, f32[1,16,32]{2,1,0:T(8,128)S(1)}, u32[]{:S(2)}, u32[]{:S(2)}) collective-permute-start(f32[1,16,32]{2,1,0:T(8,128)S(1)} %get-tuple-element.158), channel_id=1, source_target_pairs={{0,4},{4,8},{8,12},{12,16},{16,20},{20,24},{24,28},{1,5},{5,9},{9,... | collective-permute-start | bytes 6152 | tf_op jit(solution)/shard_map/ppermute | solution.py:23
  356.6 6.4 %collective-permute-start.56 = (f32[1,1,16,128]{3,2,1,0:T(8,128)S(1)}, f32[1,1,16,128]{3,2,1,0:T(8,128)S(1)}, u32[]{:S(2)}, u32[]{:S(2)}) collective-permute-start(f32[1,1,16,128]{3,2,1,0:T(8,128)S(1)} %get-tuple-element.102), channel_id=1, source_target_pairs={{0,4},{4,8},{8,12},{12,16},{16,20},{20,24},{24,28},{1,5},{5,9},{9,... | collective-permute-start | bytes 24584 | tf_op jit(solution)/shard_map/ppermute | solution.py:23
  372.4 6.4 %collective-permute-start.60 = (f32[1,1,16,128]{3,2,1,0:T(8,128)S(1)}, f32[1,1,16,128]{3,2,1,0:T(8,128)S(1)}, u32[]{:S(2)}, u32[]{:S(2)}) collective-permute-start(f32[1,1,16,128]{3,2,1,0:T(8,128)S(1)} %get-tuple-element.100), channel_id=1, source_target_pairs={{0,4},{4,8},{8,12},{12,16},{16,20},{20,24},{24,28},{1,5},{5,9},{9,... | collective-permute-start | bytes 24584 | tf_op jit(solution)/shard_map/ppermute | solution.py:23
  388.2 6.4 %collective-permute-start.64 = (f32[1,1,16,128]{3,2,1,0:T(8,128)S(1)}, f32[1,1,16,128]{3,2,1,0:T(8,128)S(1)}, u32[]{:S(2)}, u32[]{:S(2)}) collective-permute-start(f32[1,1,16,128]{3,2,1,0:T(8,128)S(1)} %get-tuple-element.98), channel_id=1, source_target_pairs={{0,4},{4,8},{8,12},{12,16},{16,20},{20,24},{24,28},{1,5},{5,9},{9,... | collective-permute-start | bytes 24584 | tf_op jit(solution)/shard_map/ppermute | solution.py:23
  (46 other events, 256.1 us)
where the time goes:
time: 405 us; the launch traced here: 403 us
  starting transfers between devices  181 us (45%)
  waiting for transfers between devices  85.1 us (21%)
  other arithmetic  69.4 us (17%)
  local copies, waits for them, and re-layouts  49.5 us (12%)
  blocking collectives  15.9 us (4%)
    ppermute x34, starting transfers between devices, padded_2(): lax.ppermute(tail, axis, [(i, (i + 1) % count) for i in range(ends)])  105 us
    ppermute x34, waiting for transfers between devices, padded_2(): lax.ppermute(tail, axis, [(i, (i + 1) % count) for i in range(ends)])  83 us
    ppermute x34, starting transfers between devices, padded_2(): lax.ppermute(head, axis, [((i + 1) % count, i) for i in range(ends)])  76.4 us
    reduce_sum x4, other arithmetic, coarsen(): return jnp.mean(split, axis=(-5, -3, -1))  36.5 us
    concatenate x1, local copies, waits for them, and re-layouts, padded_2(): jnp.concatenate([lax.ppermute(tail, axis, [(i, (i + 1) % count) for i in...  18.2 us
    another operation x3, other arithmetic, local_fields(): return jnp.stack([fields[0], fields[1], fields[2], storage])  16.5 us
    reshape x2, local copies, waits for them, and re-layouts, coarsen(): values.reshape(lead + (size_x // 2, 2, size_y // 2, 2, size_z // 2, 2))  10.9 us
    all_gather x1, blocking collectives, local(): lax.all_gather(narrow, 'gy', axis=2, tiled=True)  10.7 us
  transfers between devices with their start and end apart: 68, of which 33 were waited for; matrix products, arithmetic and copies ran while one was open for 15% of the time, Pallas kernels for 0%

commit v1 on v0

--- a/solution.py
+++ b/solution.py
@@ -10,6 +10,29 @@
 cheb_half = 0.9
 cheb_ratio = cheb_centre / cheb_half
 jacobi_weight = 0.8
+
+
+def in_order(pieces, dim):
+    pieces = jnp.moveaxis(pieces, 0, dim)
+    shape = pieces.shape
+    return pieces.reshape(*shape[:dim], shape[dim] * shape[dim + 1], *shape[dim + 2 :])
+
+
+def doubled(x, axis):
+    size, index = (lax.axis_size(axis), lax.axis_index(axis))
+    blocks, apart = (x[None], 1)
+    while apart < size:
+        received = lax.ppermute(blocks, axis, [(i, i ^ apart) for i in range(size)])
+        low = index & apart == 0
+        blocks = jnp.concatenate(
+            [jnp.where(low, blocks, received), jnp.where(low, received, blocks)]
+        )
+        apart *= 2
+    return blocks
+
+
+def collect(array, axis, dim):
+    return in_order(doubled(array, axis), dim)
 
 
 def padded_2(cells, sides, width):
@@ -172,7 +195,7 @@
     narrow = coarse_coeffs[:, :, 1:-1]
     group_source, group_coeffs = (
         lax.all_gather(coarse_source, "gy", axis=1, tiled=True),
-        lax.all_gather(narrow, "gy", axis=2, tiled=True),
+        collect(narrow, "gy", 2),
     )
     line_total = jnp.sum(group_source, axis=1)
     line_store = jnp.sum(group_coeffs[3, 1:-1], axis=1)

time: 405 us -> 392 us (0.968)
  blocking collectives: 15.9 us -> 5.19 us
    all_gather x1 -> x0, blocking collectives: 10.7 us -> none  [local(): lax.all_gather(narrow, 'gy', axis=2, tiled=True)]
    ppermute x34, starting transfers between devices: 76.4 us -> 72.1 us  [padded_2(): lax.ppermute(head, axis, [((i + 1) % count, i) for i in range(ends)])]
  transfers between devices with their start and end apart: 68 -> 70, of which waited for: 33 -> 34; matrix products, arithmetic and copies ran while one was open for 15% -> 15% of each run, Pallas kernels for 0% -> 0%
where the time goes in v1:
time: 392 us; the launch traced here: 389 us
  starting transfers between devices  179 us (46%)
  waiting for transfers between devices  87.4 us (22%)
  other arithmetic  68.7 us (18%)
  local copies, waits for them, and re-layouts  47.1 us (12%)
  blocking collectives  5.19 us (1%)
    ppermute x34, starting transfers between devices, padded_2(): lax.ppermute(tail, axis, [(i, (i + 1) % count) for i in range(ends)])  107 us
    ppermute x34, waiting for transfers between devices, padded_2(): lax.ppermute(tail, axis, [(i, (i + 1) % count) for i in range(ends)])  85.3 us
    ppermute x34, starting transfers between devices, padded_2(): lax.ppermute(head, axis, [((i + 1) % count, i) for i in range(ends)])  72.1 us
    reduce_sum x4, other arithmetic, coarsen(): return jnp.mean(split, axis=(-5, -3, -1))  36.6 us
    concatenate x1, local copies, waits for them, and re-layouts, padded_2(): jnp.concatenate([lax.ppermute(tail, axis, [(i, (i + 1) % count) for i in...  17.9 us
    another operation x3, other arithmetic, local_fields(): return jnp.stack([fields[0], fields[1], fields[2], storage])  16.1 us
    reshape x2, local copies, waits for them, and re-layouts, coarsen(): values.reshape(lead + (size_x // 2, 2, size_y // 2, 2, size_z // 2, 2))  10.8 us
    mul x1, other arithmetic, local_fields(): storage_scale * (1.0 + fields[3] * jnp.exp((fields[4] - 1.0) * jnp.log(co...  10.4 us
  transfers between devices with their start and end apart: 70, of which 34 were waited for; matrix products, arithmetic and copies ran while one was open for 15% of the time, Pallas kernels for 0%

profile of v1, /device:TPU:26, one launch (start us, length us, event | category | flops | bytes accessed | tf_op | source)
XLA Modules:
  0.0 389.3 jit_solution(14971885164743324348)
XLA Ops:
  5.5 6.0 %add_bitcast_fusion.3 = (f32[1,16,16,128]{3,2,1,0:T(8,128)S(1)}, pred[16,16,128]{2,1,0:T(8,128)(4,1)S(1)}, pred[16,16,128]{2,1,0:T(8,128)(4,1)S(1)}, pred[16,16,...) fusion(f32[]{:T(128)} %bitcast.23, f32[]{:T(128)} %bitcast.22, ...), kind=kLoop, calls=%fused_computation.161 | loop fusion | flops 753664 | bytes 524320 | tf_op jit(solution)/shard_map/stack | solution.py:176
  11.5 5.1 %add_bitcast_fusion.1 = f32[1,16,16,128]{3,2,1,0:T(8,128)S(1)} fusion(pred[16,16,128]{2,1,0:T(8,128)(4,1)S(1)} %get-tuple-element.44, pred[16,16,128]{2,1,0:T(8,128)(4,1)S(1)} %get-tuple-element.43, pred[16,16,128]{2,1,0:T(8,128)(4,1)S(1)} %get-tuple-element.42, pred[16,16,128]{2,1,0:T(8,128)(4,1)S(1)} %get-tuple-element.41, ...), kind=kLoop, calls=%fused_computation.159 | loop fusion | flops 491520 | bytes 393248 | tf_op jit(solution)/shard_map/stack | solution.py:176
  16.6 5.1 %add_bitcast_fusion.2 = f32[1,16,16,128]{3,2,1,0:T(8,128)S(1)} fusion(pred[16,16,128]{2,1,0:T(8,128)(4,1)S(1)} %get-tuple-element.44, pred[16,16,128]{2,1,0:T(8,128)(4,1)S(1)} %get-tuple-element.43, pred[16,16,128]{2,1,0:T(8,128)(4,1)S(1)} %get-tuple-element.42, pred[16,16,128]{2,1,0:T(8,128)(4,1)S(1)} %get-tuple-element.41, ...), kind=kLoop, calls=%fused_computation.160 | loop fusion | flops 491520 | bytes 393248 | tf_op jit(solution)/shard_map/stack | solution.py:176
  21.7 10.4 %add_multiply_fusion = f32[16,16,128]{2,1,0:T(8,128)S(1)} fusion(f32[16,16,128]{2,1,0:T(8,128)S(1)} %copy-done.1, pred[16,16,128]{2,1,0:T(8,128)(4,1)S(1)} %get-tuple-element.44, pred[16,16,128]{2,1,0:T(8,128)(4,1)S(1)} %get-tuple-element.43, pred[16,16,128]{2,1,0:T(8,128)(4,1)S(1)} %get-tuple-element.42, pred[16,16,128]{2,1,0:T(8,128)(4,1)S(1)} %get-tuple-element.41, ...), kind=kLoop, calls=%fused_computation.162 | loop fusion | flops 1146880 | bytes 524352 | tf_op jit(solution)/shard_map/mul | solution.py:175
  39.2 4.0 %collective-permute-done = f32[4,4,16,128]{3,2,1,0:T(8,128)S(1)} collective-permute-done((f32[4,4,16,128]{3,2,1,0:T(8,128)S(1)}, f32[4,4,16,128]{3,2,1,0:T(8,128)S(1)}, u32[]{:S(2)}, u32[]{:S(2)}) %collective-permute-start) | collective-permute-done | bytes 131104 | tf_op jit(solution)/shard_map/ppermute | solution.py:46
  59.4 17.9 %copy.584 = f32[4,24,24,128]{0,3,2,1:T(8,128)} copy(f32[4,24,24,128]{3,2,1,0:T(8,128)S(1)} %pad_maximum_fusion) | data formatting | bytes 2359296 | tf_op jit(solution)/shard_map/concatenate | solution.py:44
  77.4 27.0 %reduce_sum.55 = f32[4,12,12,64]{0,3,2,1:T(8,128)} reduce(f32[4,12,2,12,2,64,2]{0,6,5,4,3,2,1:T(2,128)} %bitcast.191, f32[]{:T(128)} %constant.27.clone.1), dimensions={2,4,6}, to_apply=%region_1.2 | reduce | flops 258048 | bytes 1327108 | tf_op jit(solution)/shard_map/reduce_sum | solution.py:108
  115.6 5.3 %reduce_sum.58 = f32[4,6,6,32]{0,3,2,1:T(8,128)S(1)} reduce(f32[4,6,2,6,2,32,2]{0,6,5,4,3,2,1:T(2,128)} %bitcast.192, f32[]{:T(128)} %constant.27.clone.1), dimensions={2,4,6}, to_apply=%region_4.5 | reduce | flops 32256 | bytes 165892 | tf_op jit(solution)/shard_map/reduce_sum | solution.py:108
  121.5 4.1 %collective-permute-start.9 = (f32[1,1,16,128]{3,2,1,0:T(8,128)S(1)}, f32[1,1,16,128]{3,2,1,0:T(8,128)S(1)}, u32[]{:S(2)}, u32[]{:S(2)}) collective-permute-start(f32[1,1,16,128]{3,2,1,0:T(8,128)S(1)} %get-tuple-element.109), channel_id=1, source_target_pairs={{4,0},{8,4},{12,8},{16,12},{20,16},{24,20},{28,24},{5,1},{9,5},{13... | collective-permute-start | bytes 24584 | tf_op jit(solution)/shard_map/ppermute | solution.py:48
  127.6 4.5 %collective-permute-done.8 = f32[1,1,16,128]{3,2,1,0:T(8,128)S(1)} collective-permute-done((f32[1,1,16,128]{3,2,1,0:T(8,128)S(1)}, f32[1,1,16,128]{3,2,1,0:T(8,128)S(1)}, u32[]{:S(2)}, u32[]{:S(2)}) %collective-permute-start.8) | collective-permute-done | bytes 8224 | tf_op jit(solution)/shard_map/ppermute | solution.py:46
  141.4 3.9 %collective-permute-start.12 = (f32[1,1,16,128]{3,2,1,0:T(8,128)S(1)}, f32[1,1,16,128]{3,2,1,0:T(8,128)S(1)}, u32[]{:S(2)}, u32[]{:S(2)}) collective-permute-start(f32[1,1,16,128]{3,2,1,0:T(8,128)S(1)} %get-tuple-element.106), channel_id=1, source_target_pairs={{0,4},{4,8},{8,12},{12,16},{16,20},{20,24},{24,28},{1,5},{5,9},{9,... | collective-permute-start | bytes 24584 | tf_op jit(solution)/shard_map/ppermute | solution.py:46
  155.3 9.8 %reshape.59 = f32[8,2,8,2,64,2]{5,4,3,2,1,0:T(8,128)} reshape(f32[16,16,128]{2,1,0:T(8,128)S(1)} %fusion.41) | data formatting | bytes 262144 | tf_op jit(solution)/shard_map/reshape | solution.py:107
  165.0 4.0 %reduce_sum.54 = f32[8,8,64]{2,1,0:T(8,128)S(1)} reduce(f32[8,2,8,2,64,2]{5,4,3,2,1,0:T(8,128)} %reshape.59, f32[]{:T(128)} %constant.27.clone.1), dimensions={1,3,5}, to_apply=%region_0.1 | reduce | flops 28672 | bytes 147460 | tf_op jit(solution)/shard_map/reduce_sum | solution.py:108
  187.6 3.9 %collective-permute-start.20 = (f32[1,1,8,64]{3,2,1,0:T(8,128)S(1)}, f32[1,1,8,64]{3,2,1,0:T(8,128)S(1)}, u32[]{:S(2)}, u32[]{:S(2)}) collective-permute-start(f32[1,1,8,64]{3,2,1,0:T(8,128)S(1)} %get-tuple-element.202), channel_id=1, source_target_pairs={{0,4},{4,8},{8,12},{12,16},{16,20},{20,24},{24,28},{1,5},{5,9},{9,... | collective-permute-start | bytes 6152 | tf_op jit(solution)/shard_map/ppermute | solution.py:46
  219.1 5.2 %all_gather.3 = f32[4,16,32]{2,0,1:T(4,128)S(1)} all-gather(f32[4,4,32]{2,0,1:T(4,128)S(1)} %copy.595), channel_id=1, replica_groups=mesh['gx'=8,'gy'=4] {'gy'}, dimensions={1}, use_global_device_ids=true | all-gather | bytes 10240 | tf_op jit(solution)/shard_map/all_gather | solution.py:197
  226.3 3.9 %collective-permute-start.31 = (f32[1,16,32]{2,1,0:T(8,128)S(1)}, f32[1,16,32]{2,1,0:T(8,128)S(1)}, u32[]{:S(2)}, u32[]{:S(2)}) collective-permute-start(f32[1,16,32]{2,1,0:T(8,128)S(1)} %broadcast_in_dim.289), channel_id=1, source_target_pairs={{0,4},{4,8},{8,12},{12,16},{16,20},{20,24},{24,28},{1,5},{5,9},{9,... | collective-permute-start | bytes 6152 | tf_op jit(solution)/shard_map/ppermute | solution.py:46
  235.1 3.9 %collective-permute-start.33 = (f32[1,16,32]{2,1,0:T(8,128)S(1)}, f32[1,16,32]{2,1,0:T(8,128)S(1)}, u32[]{:S(2)}, u32[]{:S(2)}) collective-permute-start(f32[1,16,32]{2,1,0:T(8,128)S(1)} %get-tuple-element.194), channel_id=1, source_target_pairs={{0,4},{4,8},{8,12},{12,16},{16,20},{20,24},{24,28},{1,5},{5,9},{9,... | collective-permute-start | bytes 6152 | tf_op jit(solution)/shard_map/ppermute | solution.py:46
  243.7 3.9 %collective-permute-start.35 = (f32[1,16,32]{2,1,0:T(8,128)S(1)}, f32[1,16,32]{2,1,0:T(8,128)S(1)}, u32[]{:S(2)}, u32[]{:S(2)}) collective-permute-start(f32[1,16,32]{2,1,0:T(8,128)S(1)} %get-tuple-element.188), channel_id=1, source_target_pairs={{0,4},{4,8},{8,12},{12,16},{16,20},{20,24},{24,28},{1,5},{5,9},{9,... | collective-permute-start | bytes 6152 | tf_op jit(solution)/shard_map/ppermute | solution.py:46
  252.2 3.9 %collective-permute-start.37 = (f32[1,16,32]{2,1,0:T(8,128)S(1)}, f32[1,16,32]{2,1,0:T(8,128)S(1)}, u32[]{:S(2)}, u32[]{:S(2)}) collective-permute-start(f32[1,16,32]{2,1,0:T(8,128)S(1)} %get-tuple-element.182), channel_id=1, source_target_pairs={{0,4},{4,8},{8,12},{12,16},{16,20},{20,24},{24,28},{1,5},{5,9},{9,... | collective-permute-start | bytes 6152 | tf_op jit(solution)/shard_map/ppermute | solution.py:46
  260.8 3.9 %collective-permute-start.39 = (f32[1,16,32]{2,1,0:T(8,128)S(1)}, f32[1,16,32]{2,1,0:T(8,128)S(1)}, u32[]{:S(2)}, u32[]{:S(2)}) collective-permute-start(f32[1,16,32]{2,1,0:T(8,128)S(1)} %get-tuple-element.176), channel_id=1, source_target_pairs={{0,4},{4,8},{8,12},{12,16},{16,20},{20,24},{24,28},{1,5},{5,9},{9,... | collective-permute-start | bytes 6152 | tf_op jit(solution)/shard_map/ppermute | solution.py:46
  269.4 3.9 %collective-permute-start.41 = (f32[1,16,32]{2,1,0:T(8,128)S(1)}, f32[1,16,32]{2,1,0:T(8,128)S(1)}, u32[]{:S(2)}, u32[]{:S(2)}) collective-permute-start(f32[1,16,32]{2,1,0:T(8,128)S(1)} %get-tuple-element.170), channel_id=1, source_target_pairs={{0,4},{4,8},{8,12},{12,16},{16,20},{20,24},{24,28},{1,5},{5,9},{9,... | collective-permute-start | bytes 6152 | tf_op jit(solution)/shard_map/ppermute | solution.py:46
  278.0 3.9 %collective-permute-start.43 = (f32[1,16,32]{2,1,0:T(8,128)S(1)}, f32[1,16,32]{2,1,0:T(8,128)S(1)}, u32[]{:S(2)}, u32[]{:S(2)}) collective-permute-start(f32[1,16,32]{2,1,0:T(8,128)S(1)} %get-tuple-element.164), channel_id=1, source_target_pairs={{0,4},{4,8},{8,12},{12,16},{16,20},{20,24},{24,28},{1,5},{5,9},{9,... | collective-permute-start | bytes 6152 | tf_op jit(solution)/shard_map/ppermute | solution.py:46
  326.7 3.9 %collective-permute-start.54 = (f32[1,1,8,64]{3,2,1,0:T(8,128)S(1)}, f32[1,1,8,64]{3,2,1,0:T(8,128)S(1)}, u32[]{:S(2)}, u32[]{:S(2)}) collective-permute-start(f32[1,1,8,64]{3,2,1,0:T(8,128)S(1)} %get-tuple-element.150), channel_id=1, source_target_pairs={{0,4},{4,8},{8,12},{12,16},{16,20},{20,24},{24,28},{1,5},{5,9},{9,... | collective-permute-start | bytes 6152 | tf_op jit(solution)/shard_map/ppermute | solution.py:46
  343.1 3.9 %collective-permute-start.58 = (f32[1,1,16,128]{3,2,1,0:T(8,128)S(1)}, f32[1,1,16,128]{3,2,1,0:T(8,128)S(1)}, u32[]{:S(2)}, u32[]{:S(2)}) collective-permute-start(f32[1,1,16,128]{3,2,1,0:T(8,128)S(1)} %get-tuple-element.104), channel_id=1, source_target_pairs={{0,4},{4,8},{8,12},{12,16},{16,20},{20,24},{24,28},{1,5},{5,9},{9,... | collective-permute-start | bytes 24584 | tf_op jit(solution)/shard_map/ppermute | solution.py:46
  (312 shorter events, 236.2 us)
Async XLA Ops:
  32.1 7.1 %collective-permute-start.1 = (f32[4,4,16,128]{3,2,1,0:T(8,128)S(1)}, f32[4,4,16,128]{3,2,1,0:T(8,128)S(1)}, u32[]{:S(2)}, u32[]{:S(2)}) collective-permute-start(f32[4,4,16,128]{3,2,1,0:T(8,128)S(1)} %get-tuple-element.51), channel_id=1, source_target_pairs={{4,0},{8,4},{12,8},{16,12},{20,16},{24,20},{28,24},{5,1},{9,5},{13... | collective-permute-start | bytes 393224 | tf_op jit(solution)/shard_map/ppermute | solution.py:48
  35.4 7.8 %collective-permute-start = (f32[4,4,16,128]{3,2,1,0:T(8,128)S(1)}, f32[4,4,16,128]{3,2,1,0:T(8,128)S(1)}, u32[]{:S(2)}, u32[]{:S(2)}) collective-permute-start(f32[4,4,16,128]{3,2,1,0:T(8,128)S(1)} %get-tuple-element.50), channel_id=1, source_target_pairs={{0,4},{4,8},{8,12},{12,16},{16,20},{20,24},{24,28},{1,5},{5,9},{9,... | collective-permute-start | bytes 393224 | tf_op jit(solution)/shard_map/ppermute | solution.py:46
  45.2 7.0 %collective-permute-start.2 = (f32[4,24,4,128]{3,1,2,0:T(8,128)S(1)}, f32[4,24,4,128]{3,1,2,0:T(8,128)S(1)}, u32[]{:S(2)}, u32[]{:S(2)}) collective-permute-start(f32[4,24,4,128]{3,1,2,0:T(8,128)S(1)} %copy.630), channel_id=1, source_target_pairs={{0,1},{1,2},{2,3},{4,5},{5,6},{6,7},{8,9},{9,10},{10,11},{12,13},{... | collective-permute-start | bytes 589832 | tf_op jit(solution)/shard_map/ppermute | solution.py:46
  53.6 54.6 %collective-permute-start.5 = (f32[1,1,16,128]{3,2,1,0:T(8,128)S(1)}, f32[1,1,16,128]{3,2,1,0:T(8,128)S(1)}, u32[]{:S(2)}, u32[]{:S(2)}) collective-permute-start(f32[1,1,16,128]{3,2,1,0:T(8,128)S(1)} %get-tuple-element.111), channel_id=1, source_target_pairs={{4,0},{8,4},{12,8},{16,12},{20,16},{24,20},{28,24},{5,1},{9,5},{13... | collective-permute-start | bytes 24584 | tf_op jit(solution)/shard_map/ppermute | solution.py:48
  56.8 51.4 %collective-permute-start.4 = (f32[1,1,16,128]{3,2,1,0:T(8,128)S(1)}, f32[1,1,16,128]{3,2,1,0:T(8,128)S(1)}, u32[]{:S(2)}, u32[]{:S(2)}) collective-permute-start(f32[1,1,16,128]{3,2,1,0:T(8,128)S(1)} %get-tuple-element.110), channel_id=1, source_target_pairs={{0,4},{4,8},{8,12},{12,16},{16,20},{20,24},{24,28},{1,5},{5,9},{9,... | collective-permute-start | bytes 24584 | tf_op jit(solution)/shard_map/ppermute | solution.py:46
  108.2 12.8 %collective-permute-start.7 = (f32[1,18,1,128]{3,2,1,0:T(1,128)S(1)}, f32[1,18,1,128]{3,2,1,0:T(1,128)S(1)}, u32[]{:S(2)}, u32[]{:S(2)}) collective-permute-start(f32[1,18,1,128]{3,2,1,0:T(1,128)S(1)} %get-tuple-element.99), channel_id=1, source_target_pairs={{1,0},{2,1},{3,2},{5,4},{6,5},{7,6},{9,8},{10,9},{11,10},{13,12},{... | collective-permute-start | bytes 27656 | tf_op jit(solution)/shard_map/ppermute | solution.py:48
  110.1 10.9 %collective-permute-start.6 = (f32[1,18,1,128]{3,2,1,0:T(1,128)S(1)}, f32[1,18,1,128]{3,2,1,0:T(1,128)S(1)}, u32[]{:S(2)}, u32[]{:S(2)}) collective-permute-start(f32[1,18,1,128]{3,2,1,0:T(1,128)S(1)} %get-tuple-element.98), channel_id=1, source_target_pairs={{0,1},{1,2},{2,3},{4,5},{5,6},{6,7},{8,9},{9,10},{10,11},{12,13},{... | collective-permute-start | bytes 27656 | tf_op jit(solution)/shard_map/ppermute | solution.py:46
  125.6 6.4 %collective-permute-start.8 = (f32[1,1,16,128]{3,2,1,0:T(8,128)S(1)}, f32[1,1,16,128]{3,2,1,0:T(8,128)S(1)}, u32[]{:S(2)}, u32[]{:S(2)}) collective-permute-start(f32[1,1,16,128]{3,2,1,0:T(8,128)S(1)} %get-tuple-element.108), channel_id=1, source_target_pairs={{0,4},{4,8},{8,12},{12,16},{16,20},{20,24},{24,28},{1,5},{5,9},{9,... | collective-permute-start | bytes 24584 | tf_op jit(solution)/shard_map/ppermute | solution.py:46
  141.4 6.4 %collective-permute-start.12 = (f32[1,1,16,128]{3,2,1,0:T(8,128)S(1)}, f32[1,1,16,128]{3,2,1,0:T(8,128)S(1)}, u32[]{:S(2)}, u32[]{:S(2)}) collective-permute-start(f32[1,1,16,128]{3,2,1,0:T(8,128)S(1)} %get-tuple-element.106), channel_id=1, source_target_pairs={{0,4},{4,8},{8,12},{12,16},{16,20},{20,24},{24,28},{1,5},{5,9},{9,... | collective-permute-start | bytes 24584 | tf_op jit(solution)/shard_map/ppermute | solution.py:46
  145.7 6.8 %collective-permute-start.28 = (f32[1,4,6,4,32]{4,3,2,1,0:T(4,128)S(1)}, f32[1,4,6,4,32]{4,3,2,1,0:T(4,128)S(1)}, u32[]{:S(2)}, u32[]{:S(2)}) collective-permute-start(f32[1,4,6,4,32]{4,3,2,1,0:T(4,128)S(1)} %bitcast.241), channel_id=1, source_target_pairs={{0,1},{1,0},{2,3},{3,2},{4,5},{5,4},{6,7},{7,6},{8,9},{9,8},{10,11... | collective-permute-start | bytes 36872 | tf_op jit(solution)/shard_map/ppermute | solution.py:25
  172.1 6.4 %collective-permute-start.16 = (f32[1,1,8,64]{3,2,1,0:T(8,128)S(1)}, f32[1,1,8,64]{3,2,1,0:T(8,128)S(1)}, u32[]{:S(2)}, u32[]{:S(2)}) collective-permute-start(f32[1,1,8,64]{3,2,1,0:T(8,128)S(1)} %get-tuple-element.204), channel_id=1, source_target_pairs={{0,4},{4,8},{8,12},{12,16},{16,20},{20,24},{24,28},{1,5},{5,9},{9,... | collective-permute-start | bytes 6152 | tf_op jit(solution)/shard_map/ppermute | solution.py:46
  175.1 7.8 %collective-permute-start.29 = (f32[2,4,6,4,32]{4,3,2,1,0:T(4,128)S(1)}, f32[2,4,6,4,32]{4,3,2,1,0:T(4,128)S(1)}, u32[]{:S(2)}, u32[]{:S(2)}) collective-permute-start(f32[2,4,6,4,32]{4,3,2,1,0:T(4,128)S(1)} %pad_maximum_fusion.11), channel_id=1, source_target_pairs={{0,2},{1,3},{2,0},{3,1},{4,6},{5,7},{6,4},{7,5},{8,10},{9,11},{10,... | collective-permute-start | bytes 73736 | tf_op jit(solution)/shard_map/ppermute | solution.py:25
  187.6 6.4 %collective-permute-start.20 = (f32[1,1,8,64]{3,2,1,0:T(8,128)S(1)}, f32[1,1,8,64]{3,2,1,0:T(8,128)S(1)}, u32[]{:S(2)}, u32[]{:S(2)}) collective-permute-start(f32[1,1,8,64]{3,2,1,0:T(8,128)S(1)} %get-tuple-element.202), channel_id=1, source_target_pairs={{0,4},{4,8},{8,12},{12,16},{16,20},{20,24},{24,28},{1,5},{5,9},{9,... | collective-permute-start | bytes 6152 | tf_op jit(solution)/shard_map/ppermute | solution.py:46
  226.3 6.4 %collective-permute-start.31 = (f32[1,16,32]{2,1,0:T(8,128)S(1)}, f32[1,16,32]{2,1,0:T(8,128)S(1)}, u32[]{:S(2)}, u32[]{:S(2)}) collective-permute-start(f32[1,16,32]{2,1,0:T(8,128)S(1)} %broadcast_in_dim.289), channel_id=1, source_target_pairs={{0,4},{4,8},{8,12},{12,16},{16,20},{20,24},{24,28},{1,5},{5,9},{9,... | collective-permute-start | bytes 6152 | tf_op jit(solution)/shard_map/ppermute | solution.py:46
  235.1 6.4 %collective-permute-start.33 = (f32[1,16,32]{2,1,0:T(8,128)S(1)}, f32[1,16,32]{2,1,0:T(8,128)S(1)}, u32[]{:S(2)}, u32[]{:S(2)}) collective-permute-start(f32[1,16,32]{2,1,0:T(8,128)S(1)} %get-tuple-element.194), channel_id=1, source_target_pairs={{0,4},{4,8},{8,12},{12,16},{16,20},{20,24},{24,28},{1,5},{5,9},{9,... | collective-permute-start | bytes 6152 | tf_op jit(solution)/shard_map/ppermute | solution.py:46
  243.7 6.4 %collective-permute-start.35 = (f32[1,16,32]{2,1,0:T(8,128)S(1)}, f32[1,16,32]{2,1,0:T(8,128)S(1)}, u32[]{:S(2)}, u32[]{:S(2)}) collective-permute-start(f32[1,16,32]{2,1,0:T(8,128)S(1)} %get-tuple-element.188), channel_id=1, source_target_pairs={{0,4},{4,8},{8,12},{12,16},{16,20},{20,24},{24,28},{1,5},{5,9},{9,... | collective-permute-start | bytes 6152 | tf_op jit(solution)/shard_map/ppermute | solution.py:46
  252.2 6.4 %collective-permute-start.37 = (f32[1,16,32]{2,1,0:T(8,128)S(1)}, f32[1,16,32]{2,1,0:T(8,128)S(1)}, u32[]{:S(2)}, u32[]{:S(2)}) collective-permute-start(f32[1,16,32]{2,1,0:T(8,128)S(1)} %get-tuple-element.182), channel_id=1, source_target_pairs={{0,4},{4,8},{8,12},{12,16},{16,20},{20,24},{24,28},{1,5},{5,9},{9,... | collective-permute-start | bytes 6152 | tf_op jit(solution)/shard_map/ppermute | solution.py:46
  260.8 6.4 %collective-permute-start.39 = (f32[1,16,32]{2,1,0:T(8,128)S(1)}, f32[1,16,32]{2,1,0:T(8,128)S(1)}, u32[]{:S(2)}, u32[]{:S(2)}) collective-permute-start(f32[1,16,32]{2,1,0:T(8,128)S(1)} %get-tuple-element.176), channel_id=1, source_target_pairs={{0,4},{4,8},{8,12},{12,16},{16,20},{20,24},{24,28},{1,5},{5,9},{9,... | collective-permute-start | bytes 6152 | tf_op jit(solution)/shard_map/ppermute | solution.py:46
  269.4 6.4 %collective-permute-start.41 = (f32[1,16,32]{2,1,0:T(8,128)S(1)}, f32[1,16,32]{2,1,0:T(8,128)S(1)}, u32[]{:S(2)}, u32[]{:S(2)}) collective-permute-start(f32[1,16,32]{2,1,0:T(8,128)S(1)} %get-tuple-element.170), channel_id=1, source_target_pairs={{0,4},{4,8},{8,12},{12,16},{16,20},{20,24},{24,28},{1,5},{5,9},{9,... | collective-permute-start | bytes 6152 | tf_op jit(solution)/shard_map/ppermute | solution.py:46
  278.0 6.5 %collective-permute-start.43 = (f32[1,16,32]{2,1,0:T(8,128)S(1)}, f32[1,16,32]{2,1,0:T(8,128)S(1)}, u32[]{:S(2)}, u32[]{:S(2)}) collective-permute-start(f32[1,16,32]{2,1,0:T(8,128)S(1)} %get-tuple-element.164), channel_id=1, source_target_pairs={{0,4},{4,8},{8,12},{12,16},{16,20},{20,24},{24,28},{1,5},{5,9},{9,... | collective-permute-start | bytes 6152 | tf_op jit(solution)/shard_map/ppermute | solution.py:46
  286.7 6.4 %collective-permute-start.45 = (f32[1,16,32]{2,1,0:T(8,128)S(1)}, f32[1,16,32]{2,1,0:T(8,128)S(1)}, u32[]{:S(2)}, u32[]{:S(2)}) collective-permute-start(f32[1,16,32]{2,1,0:T(8,128)S(1)} %get-tuple-element.162), channel_id=1, source_target_pairs={{0,4},{4,8},{8,12},{12,16},{16,20},{20,24},{24,28},{1,5},{5,9},{9,... | collective-permute-start | bytes 6152 | tf_op jit(solution)/shard_map/ppermute | solution.py:46
  343.1 6.4 %collective-permute-start.58 = (f32[1,1,16,128]{3,2,1,0:T(8,128)S(1)}, f32[1,1,16,128]{3,2,1,0:T(8,128)S(1)}, u32[]{:S(2)}, u32[]{:S(2)}) collective-permute-start(f32[1,1,16,128]{3,2,1,0:T(8,128)S(1)} %get-tuple-element.104), channel_id=1, source_target_pairs={{0,4},{4,8},{8,12},{12,16},{16,20},{20,24},{24,28},{1,5},{5,9},{9,... | collective-permute-start | bytes 24584 | tf_op jit(solution)/shard_map/ppermute | solution.py:46
  358.9 6.4 %collective-permute-start.62 = (f32[1,1,16,128]{3,2,1,0:T(8,128)S(1)}, f32[1,1,16,128]{3,2,1,0:T(8,128)S(1)}, u32[]{:S(2)}, u32[]{:S(2)}) collective-permute-start(f32[1,1,16,128]{3,2,1,0:T(8,128)S(1)} %get-tuple-element.102), channel_id=1, source_target_pairs={{0,4},{4,8},{8,12},{12,16},{16,20},{20,24},{24,28},{1,5},{5,9},{9,... | collective-permute-start | bytes 24584 | tf_op jit(solution)/shard_map/ppermute | solution.py:46
  374.7 6.4 %collective-permute-start.66 = (f32[1,1,16,128]{3,2,1,0:T(8,128)S(1)}, f32[1,1,16,128]{3,2,1,0:T(8,128)S(1)}, u32[]{:S(2)}, u32[]{:S(2)}) collective-permute-start(f32[1,1,16,128]{3,2,1,0:T(8,128)S(1)} %get-tuple-element.100), channel_id=1, source_target_pairs={{0,4},{4,8},{8,12},{12,16},{16,20},{20,24},{24,28},{1,5},{5,9},{9,... | collective-permute-start | bytes 24584 | tf_op jit(solution)/shard_map/ppermute | solution.py:46
  (48 other events, 268.8 us)
